TPU v7x, 512 devices: a whole 4x8x8 slice. The times are simulated.
512 devices in a mesh: seq: 128 (over z_hi, x, y), dp: 4 (over z_lo, core).
Axes of the slice: x: 4, y: 8, z: 8 (z_hi: 4, z_lo: 2; z = z_hi * 2 + z_lo), core: 2. Of those that a mesh axis runs over, the one named last changes fastest.
Arguments:
- query_proj: bfloat16 [4, 16384, 2048], P('dp', 'seq'), may hold values from -48 to 48
- key_projection: bfloat16 [4, 16384, 1024], P('dp', 'seq'), may hold values from -48 to 48
- value_proj: bfloat16 [4, 16384, 1024], P('dp', 'seq'), may hold values from -6 to 6
- attn_grad: bfloat16 [4, 16384, 2048], P('dp', 'seq'), may hold values from -6 to 6
- doc_ids: int32 [4, 16384], P('dp', 'seq'), may hold values from 0 to 8, as said below
- query_gain: float32 [128], replicated, may hold values from 0.5 to 1.5
- key_norm_gain: float32 [128], replicated, may hold values from 0.5 to 1.5
Outputs:
- query_grad: bfloat16 [4, 16384, 2048], P('dp', 'seq')
- key_grad: bfloat16 [4, 16384, 1024], P('dp', 'seq')
- value_grad: bfloat16 [4, 16384, 1024], P('dp', 'seq')
- query_gain_grad: float32 [128], replicated
- key_gain_grad: float32 [128], replicated
Inputs may be any that keep to these rules, and one draw needn't show every extreme that they name: `doc_ids`: document numbers never fall along a sequence and each is used; each document holds 1 to 2175 tokens, and one holds exactly 2175.
All inputs are finite; a program needn't handle non-finite values.
Results may differ from a plain program's by a relative error of at most 0.008.
Values may be sent and summed in bfloat16 or wider, within the bound.
No kernel may reach another device: no remote copies, remote signals or barrier semaphores. Data moves between devices by JAX's collectives and lax.ppermute only.
A program may use at most 128 MiB of HBM per device.

v0:
```python
import jax
import jax.numpy as jnp
from jax import lax
from jax.sharding import PartitionSpec as P

HEAD_SIZE = 128
QUERY_HEADS = 16
KEY_VALUE_HEADS = 8
WINDOW_LENGTH = 1024
rope_base = 10000.0
score_scale = 168.0 ** (-0.5)
norm_eps = 1e-06


def entering(value, axis, combine, identity):
    length, position = (lax.axis_size(axis), lax.axis_index(axis))
    everything = jax.tree.map(lambda part: lax.all_gather(part, axis), value)
    start = jax.tree.map(
        lambda part, zero: jnp.broadcast_to(jnp.asarray(zero, part.dtype), part.shape),
        value,
        identity,
    )

    def turn(k, before):
        reached = k < position
        new = combine(before, jax.tree.map(lambda part: part[k], everything))
        return jax.tree.map(lambda a, b: jnp.where(reached, a, b), new, before)

    return lax.fori_loop(0, length, turn, start)


def from_behind(value, axis, steps):
    count = lax.axis_size(axis)
    first, last = (max(0, -steps), min(count, count - steps))
    return lax.ppermute(value, axis, [(source, source + steps) for source in range(first, last)])


def rotary(field, positions):
    half = field.shape[-1] // 2
    freqs = rope_base ** (-jnp.arange(half, dtype=field.dtype) * 2.0 / field.shape[-1])
    angles = positions.astype(field.dtype)[:, None] * freqs[None, :]
    cosine = jnp.cos(angles)[:, None, :]
    sine = jnp.sin(angles)[:, None, :]
    first = field[..., :half]
    second = field[..., half:]
    return jnp.concatenate(
        [first * cosine - second * sine, second * cosine + first * sine], axis=-1
    )


def prepare(raw, gain, positions):
    meansq = jnp.mean(raw * raw, axis=-1, keepdims=True)
    normed = raw * lax.rsqrt(meansq + norm_eps) * gain
    return rotary(normed, positions)


def combine_docs(earlier, later):
    vacant = later[0] < 0
    joined = later[0] == earlier[0]
    doc_number = jnp.where(vacant, earlier[0], later[0])
    first_place = jnp.where(vacant | joined, earlier[1], later[1])
    return (doc_number, first_place)


def attend(query_blk, key_blk, value_blk, gradient_block, allowed):
    scores = (
        jnp.einsum("tgrd,wgd->grtw", query_blk, key_blk, preferred_element_type=jnp.float32)
        * score_scale
    )
    expd = jnp.where(allowed, jnp.exp(scores), 0.0)
    weights = expd / jnp.sum(expd, axis=-1, keepdims=True)
    weights_b = weights.astype(jnp.bfloat16)
    attention_probs = jnp.einsum(
        "grtw,wgd->tgrd", weights_b, value_blk, preferred_element_type=jnp.float32
    )
    delta_rows = jnp.einsum("jwkp,jwkp->wkj", gradient_block.astype(jnp.float32), attention_probs)
    dweights = jnp.einsum(
        "tgrd,wgd->grtw", gradient_block, value_blk, preferred_element_type=jnp.float32
    )
    dscores = (weights * (dweights - delta_rows[..., None])).astype(jnp.bfloat16)
    dquery = score_scale * jnp.einsum(
        "grtw,wgd->tgrd", dscores, key_blk, preferred_element_type=jnp.float32
    )
    dkey = score_scale * jnp.einsum(
        "grtw,tgrd->wgd", dscores, query_blk, preferred_element_type=jnp.float32
    )
    dvalue = jnp.einsum(
        "grtw,tgrd->wgd", weights_b, gradient_block, preferred_element_type=jnp.float32
    )
    return (dquery, dkey, dvalue)


def shards(query_proj, key_projection, value_proj, attn_grad, doc_ids, query_gain, key_norm_gain):
    row_count = query_proj.shape[1]
    behind = WINDOW_LENGTH // row_count
    group_ratio = QUERY_HEADS // KEY_VALUE_HEADS
    group_count = KEY_VALUE_HEADS // 2
    key_span_width = KEY_VALUE_HEADS * HEAD_SIZE
    base = lax.axis_index("seq") * row_count
    local = jnp.arange(row_count, dtype=jnp.int32)
    positions = base + local
    doc_row = doc_ids[0]
    same_doc = doc_row[:, None] == doc_row[None, :]
    local_first = jnp.min(jnp.where(same_doc, local[None, :], row_count), axis=1) + base
    carry_doc, carry_start = entering(
        (doc_row[row_count - 1], local_first[row_count - 1]),
        "seq",
        combine_docs,
        (jnp.int32(-1), jnp.int32(0)),
    )
    starts = jnp.where(doc_row == carry_doc, carry_start, local_first)

    def prepare_function(raw, gain):
        return prepare(raw, gain, positions)

    query_normalized, query_back = jax.vjp(
        prepare_function,
        query_proj[0].astype(jnp.float32).reshape(row_count, QUERY_HEADS, HEAD_SIZE),
        query_gain,
    )
    key_normalized, key_backward = jax.vjp(
        prepare_function,
        key_projection[0].astype(jnp.float32).reshape(row_count, KEY_VALUE_HEADS, HEAD_SIZE),
        key_norm_gain,
    )
    query_rot = query_normalized.astype(jnp.bfloat16)
    key_flat = key_normalized.astype(jnp.bfloat16).reshape(row_count, key_span_width)
    value_flat = value_proj[0]
    key_parts = []
    value_parts = []
    for offset in range(behind, 0, -1):
        moved = from_behind((key_flat, value_flat), "seq", offset)
        key_parts.append(moved[0])
        value_parts.append(moved[1])
    key_win = jnp.concatenate(key_parts + [key_flat], axis=0)
    value_win = jnp.concatenate(value_parts + [value_flat], axis=0)
    width = (behind + 1) * row_count
    key_pos = base - behind * row_count + jnp.arange(width, dtype=jnp.int32)
    allowed = (
        (key_pos[None, :] <= positions[:, None])
        & (positions[:, None] - key_pos[None, :] < WINDOW_LENGTH)
        & (key_pos[None, :] >= starts[:, None])
    )
    query_groups = query_rot.reshape(row_count, group_count, 2, group_ratio, HEAD_SIZE).transpose(
        1, 0, 2, 3, 4
    )
    grad_groups = (
        attn_grad[0]
        .reshape(row_count, group_count, 2, group_ratio, HEAD_SIZE)
        .transpose(1, 0, 2, 3, 4)
    )
    key_groups = key_win.reshape(width, group_count, 2, HEAD_SIZE).transpose(1, 0, 2, 3)
    value_groups = value_win.reshape(width, group_count, 2, HEAD_SIZE).transpose(1, 0, 2, 3)

    def group_work(items):
        return attend(items[0], items[1], items[2], items[3], allowed)

    dquery_g, dkey_g, dvalue_g = lax.map(
        group_work, (query_groups, key_groups, value_groups, grad_groups)
    )
    dquery_rot = dquery_g.transpose(1, 0, 2, 3, 4).reshape(row_count, QUERY_HEADS, HEAD_SIZE)
    dkey_win = dkey_g.transpose(1, 0, 2, 3).reshape(behind + 1, row_count, key_span_width)
    dvalue_win = dvalue_g.transpose(1, 0, 2, 3).reshape(behind + 1, row_count, key_span_width)
    key_remote = dkey_win[:behind].astype(jnp.bfloat16)
    value_remote = dvalue_win[:behind].astype(jnp.bfloat16)
    key_full_length = dkey_win[behind]
    value_total = dvalue_win[behind]
    for offset in range(1, behind + 1):
        moved = from_behind(
            (key_remote[behind - offset], value_remote[behind - offset]), "seq", -offset
        )
        key_full_length = key_full_length + moved[0].astype(jnp.float32)
        value_total = value_total + moved[1].astype(jnp.float32)
    query_raw_gradient, query_gain_gradient = query_back(dquery_rot)
    key_raw_gradient, key_gain_gradient = key_backward(
        key_full_length.reshape(row_count, KEY_VALUE_HEADS, HEAD_SIZE)
    )
    gain_query, gain_key = lax.psum((query_gain_gradient, key_gain_gradient), ("seq", "dp"))
    return (
        query_raw_gradient.astype(jnp.bfloat16).reshape(1, row_count, QUERY_HEADS * HEAD_SIZE),
        key_raw_gradient.astype(jnp.bfloat16).reshape(1, row_count, key_span_width),
        value_total.astype(jnp.bfloat16)[None],
        gain_query,
        gain_key,
    )


def solution(mesh):
    in_specs = (
        P("dp", "seq", None),
        P("dp", "seq", None),
        P("dp", "seq", None),
        P("dp", "seq", None),
        P("dp", "seq"),
        P(),
        P(),
    )
    out_specs = (P("dp", "seq", None), P("dp", "seq", None), P("dp", "seq", None), P(), P())
    return jax.shard_map(shards, mesh=mesh, in_specs=in_specs, out_specs=out_specs, check_vma=False)
```

profile of v0, /device:TPU:1, one launch (start us, length us, event | category | flops | bytes accessed | tf_op | source)
XLA Modules:
  0.0 1063.3 jit_solution(8678204765822)
XLA Ops:
  1.8 4.0 collective-permute-start.15
  5.8 4.2 collective-permute-start.14
  10.1 3.1 collective-permute-start.8
  16.6 4.9 collective-permute-start.1
  21.5 2.9 collective-permute-start
  28.5 28.4 %all-reduce.6 = (s32[128]{0:T(128)S(1)}, s32[128]{0:T(128)S(1)}) all-reduce(s32[128]{0:T(128)S(1)} %bitcast_dynamic-update-slice_fusion, s32[128]{0:T(128)S(1)} %slice_dynamic-update-slice_fusion), channel_id=2, replica_groups=mesh['seq'=128,'dp'=4] {'seq'}, use_global_device_ids=true, to_apply=%add.4 | all-reduce | flops 256 | bytes 2048 | tf_op jit(solution)/shard_map/all_gather | solution.py:17
  57.0 487.3 %while.30 = (s32[]{:T(128)}, s32[]{:T(128)}, s32[]{:T(128)}, s32[]{:T(128)}, s32[128]{0:T(128)S(1)}, /*index=5*/s32[128]{0:T(128)S(1)}, s32[]{:T(128)}, s32[]{:T(128)}) while((s32[]{:T(128)}, s32[]{:T(128)}, s32[]{:T(128)}, s32[]{:T(128)}, s32[128]{0:T(128)S(1)}, /*index=5*/s32[128]{0:T(128)S(1)}, s32[]{:T(128)}, s32[]{:T(128)}) %tuple.77), condition=%wide.region_4.5_spmd, body=%wide.region_3.4_spmd.sunk | while | flops 10 | bytes 199 | solution.py:29
  548.3 9.9 collective-permute-start.2
  562.9 7.1 collective-permute-done.2
  571.3 20.7 %collective-permute-done.3 = bf16[128,1024]{0,1:T(8,128)(2,1)S(1)} collective-permute-done((bf16[128,1024]{0,1:T(8,128)(2,1)S(1)}, bf16[128,1024]{0,1:T(8,128)(2,1)S(1)}, u32[]{:S(2)}, u32[]{:S(2)}) %collective-permute-start.3) | collective-permute-done | bytes 262176 | tf_op jit(solution)/shard_map/ppermute | solution.py:35
  594.8 8.5 collective-permute-start.11
  603.4 10.8 %collective-permute-start.9 = (bf16[128,1024]{0,1:T(8,128)(2,1)S(1)}, bf16[128,1024]{0,1:T(8,128)(2,1)S(1)}, u32[]{:S(2)}, u32[]{:S(2)}) collective-permute-start(bf16[128,1024]{0,1:T(8,128)(2,1)S(1)} %bitcast.260), channel_id=1, source_target_pairs={{0,28},{4,32},{8,36},{12,40},{16,44},{20,48},{24,52},{28,56},{32,6... | collective-permute-start | bytes 786440 | tf_op jit(solution)/shard_map/ppermute | solution.py:35
  615.2 9.4 collective-permute-start.10
  624.7 12.8 %collective-permute-start.12 = (bf16[128,1024]{0,1:T(8,128)(2,1)S(1)}, bf16[128,1024]{0,1:T(8,128)(2,1)S(1)}, u32[]{:S(2)}, u32[]{:S(2)}) collective-permute-start(bf16[128,1024]{0,1:T(8,128)(2,1)S(1)} %bitcast.262), channel_id=1, source_target_pairs={{0,16},{4,20},{8,24},{12,28},{16,32},{20,36},{24,40},{28,44},{32,4... | collective-permute-start | bytes 786440 | tf_op jit(solution)/shard_map/ppermute | solution.py:35
  639.3 2.7 collective-permute-done.12
  642.1 4.4 collective-permute-done.13
  648.2 57.1 %while.31 = (s32[]{:T(128)}, f32[4,128,2,2,128]{1,4,3,2,0:T(8,128)}, f32[4,1152,2,128]{1,3,2,0:T(8,128)}, f32[4,1152,2,128]{1,3,2,0:T(8,128)}, bf16[4,1152,2,128...) while((s32[]{:T(128)}, ...), condition=%wide.region_7.8_spmd.clone, body=%wide.region_5.7_spmd.clone.sunk | while | flops 912131200 | bytes 24730428 | solution.py:158
  650.2 1.9 fusion.96
  653.7 1.6 fusion.98
  655.3 2.1 fusion.99
  657.5 2.4 fusion.101
  659.9 2.5 fusion.100
  664.6 1.9 fusion.96
  669.6 2.1 fusion.99
  671.8 2.4 fusion.101
  674.2 2.5 fusion.100
  678.8 1.9 fusion.96
  683.9 2.1 fusion.99
  686.0 2.5 fusion.101
  688.5 2.5 fusion.100
  693.1 1.9 fusion.96
  698.2 2.1 fusion.99
  700.3 2.4 fusion.101
  702.8 2.5 fusion.100
  708.0 4.1 bitcast_convert_fusion.2
  712.1 1.9 slice.144
  713.9 4.1 bitcast_convert_fusion.1
  721.5 1.8 multiply_add_fusion.1
  724.5 2.9 fusion.55
  731.2 1.8 fusion.41
  733.0 2.1 reshape.221
  737.7 20.8 %collective-permute-done.23 = bf16[128,1024]{0,1:T(8,128)(2,1)} collective-permute-done((bf16[128,1024]{0,1:T(8,128)(2,1)}, bf16[128,1024]{0,1:T(8,128)(2,1)}, u32[]{:S(2)}, u32[]{:S(2)}) %collective-permute-start.23) | collective-permute-done | bytes 262176 | tf_op jit(solution)/shard_map/ppermute | solution.py:35
  761.1 38.7 %collective-permute-done.22 = bf16[128,1024]{0,1:T(8,128)(2,1)} collective-permute-done((bf16[128,1024]{0,1:T(8,128)(2,1)}, bf16[128,1024]{0,1:T(8,128)(2,1)}, u32[]{:S(2)}, u32[]{:S(2)}) %collective-permute-start.22) | collective-permute-done | bytes 262176 | tf_op jit(solution)/shard_map/ppermute | solution.py:35
  801.1 1.7 fusion.54
  819.3 6.8 collective-permute-done.25
  827.5 4.6 collective-permute-done.26
  836.1 224.7 %all-reduce.7 = (f32[128]{0:T(128)}, f32[128]{0:T(128)}) all-reduce(f32[128]{0:T(128)S(1)} %get-tuple-element.251, f32[128]{0:T(128)S(1)} %get-tuple-element.253), channel_id=1, replica_groups=mesh['seq'=128,'dp'=4] {'seq','dp'}, use_global_device_ids=true, to_apply=%region_11.12 | all-reduce | flops 256 | bytes 2048 | tf_op jit(solution)/shard_map/psum | solution.py:178
  1060.8 2.5 fusion.50
  (520 shorter events, 234.4 us)
Async XLA Ops:
  0.6 15.0 %copy-start.32 = (f32[128]{0:T(128)S(1)}, f32[128]{0:T(128)}, u32[]{:S(2)}) copy-start(f32[128]{0:T(128)} %param.17) | copy-start | bytes 1540
  1.8 644.8 %collective-permute-start.15 = (bf16[128,1024]{0,1:T(8,128)(2,1)S(1)}, bf16[128,1024]{0,1:T(8,128)(2,1)S(1)}, u32[]{:S(2)}, u32[]{:S(2)}) collective-permute-start(bf16[128,1024]{0,1:T(8,128)(2,1)S(1)} %bitcast.256), channel_id=1, source_target_pairs={{0,4},{4,8},{8,12},{12,16},{16,20},{20,24},{24,28},{28,32},{32,36}... | collective-permute-start | bytes 786440 | tf_op jit(solution)/shard_map/ppermute | solution.py:35
  5.8 640.7 %collective-permute-start.14 = (bf16[128,1024]{0,1:T(8,128)(2,1)S(1)}, bf16[128,1024]{0,1:T(8,128)(2,1)S(1)}, u32[]{:S(2)}, u32[]{:S(2)}) collective-permute-start(bf16[128,1024]{0,1:T(8,128)(2,1)S(1)} %bitcast.257), channel_id=1, source_target_pairs={{0,8},{4,12},{8,16},{12,20},{16,24},{20,28},{24,32},{28,36},{32,40... | collective-permute-start | bytes 786440 | tf_op jit(solution)/shard_map/ppermute | solution.py:35
  10.1 549.1 %collective-permute-start.8 = (bf16[128,1024]{0,1:T(8,128)(2,1)S(1)}, bf16[128,1024]{0,1:T(8,128)(2,1)S(1)}, u32[]{:S(2)}, u32[]{:S(2)}) collective-permute-start(bf16[128,1024]{0,1:T(8,128)(2,1)S(1)} %bitcast.258), channel_id=1, source_target_pairs={{0,32},{4,36},{8,40},{12,44},{16,48},{20,52},{24,56},{28,60},{32,6... | collective-permute-start | bytes 786440 | tf_op jit(solution)/shard_map/ppermute | solution.py:35
  15.1 9.2 copy-start.34
  15.1 529.1 %copy-start.16 = (bf16[1,128,2048]{2,1,0:T(8,128)(2,1)S(1)}, bf16[1,128,2048]{2,1,0:T(8,128)(2,1)}, u32[]{:S(2)}) copy-start(bf16[1,128,2048]{2,1,0:T(8,128)(2,1)} %param.11) | copy-start | bytes 1572868
  15.2 529.2 %copy-start.24 = (f32[128,8]{0,1:T(8,128)}, f32[128,8]{0,1:T(8,128)S(1)}, u32[]{:S(2)}) copy-start(f32[128,8]{0,1:T(8,128)S(1)} %copy.167) | copy-start | bytes 12292
  15.3 528.9 %copy-start.14 = (f32[128,8]{1,0:T(8,128)}, f32[128,8]{1,0:T(8,128)S(1)}, u32[]{:S(2)}) copy-start(f32[128,8]{1,0:T(8,128)S(1)} %copy.168) | copy-start | bytes 12292
  15.7 529.8 %copy-start.8 = (f32[128,64]{1,0:T(8,128)}, f32[128,64]{1,0:T(8,128)S(1)}, u32[]{:S(2)}) copy-start(f32[128,64]{1,0:T(8,128)S(1)} %get-tuple-element.321) | copy-start | bytes 98308
  15.7 529.8 %copy-start.10 = (f32[128,64]{1,0:T(8,128)}, f32[128,64]{1,0:T(8,128)S(1)}, u32[]{:S(2)}) copy-start(f32[128,64]{1,0:T(8,128)S(1)} %get-tuple-element.322) | copy-start | bytes 98308
  16.6 544.0 %collective-permute-start.1 = (bf16[128,1024]{0,1:T(8,128)(2,1)S(1)}, bf16[128,1024]{0,1:T(8,128)(2,1)}, u32[]{:S(2)}, u32[]{:S(2)}) collective-permute-start(bf16[128,1024]{0,1:T(8,128)(2,1)S(1)} %bitcast.265), channel_id=1, source_target_pairs={{0,28},{4,32},{8,36},{12,40},{16,44},{20,48},{24,52},{28,56},{32,6... | collective-permute-start | bytes 786440 | tf_op jit(solution)/shard_map/ppermute | solution.py:35
  21.5 526.8 %collective-permute-start = (bf16[128,1024]{0,1:T(8,128)(2,1)S(1)}, bf16[128,1024]{0,1:T(8,128)(2,1)}, u32[]{:S(2)}, u32[]{:S(2)}) collective-permute-start(bf16[128,1024]{0,1:T(8,128)(2,1)S(1)} %bitcast.266), channel_id=1, source_target_pairs={{0,32},{4,36},{8,40},{12,44},{16,48},{20,52},{24,56},{28,60},{32,6... | collective-permute-start | bytes 786440 | tf_op jit(solution)/shard_map/ppermute | solution.py:35
  548.3 21.7 %collective-permute-start.2 = (bf16[128,1024]{0,1:T(8,128)(2,1)S(1)}, bf16[128,1024]{0,1:T(8,128)(2,1)S(1)}, u32[]{:S(2)}, u32[]{:S(2)}) collective-permute-start(bf16[128,1024]{0,1:T(8,128)(2,1)S(1)} %bitcast.267), channel_id=1, source_target_pairs={{0,24},{4,28},{8,32},{12,36},{16,40},{20,44},{24,48},{28,52},{32,5... | collective-permute-start | bytes 786440 | tf_op jit(solution)/shard_map/ppermute | solution.py:35
  559.2 32.9 %collective-permute-start.3 = (bf16[128,1024]{0,1:T(8,128)(2,1)S(1)}, bf16[128,1024]{0,1:T(8,128)(2,1)S(1)}, u32[]{:S(2)}, u32[]{:S(2)}) collective-permute-start(bf16[128,1024]{0,1:T(8,128)(2,1)S(1)} %bitcast.268), channel_id=1, source_target_pairs={{0,20},{4,24},{8,28},{12,32},{16,36},{20,40},{24,44},{28,48},{32,5... | collective-permute-start | bytes 786440 | tf_op jit(solution)/shard_map/ppermute | solution.py:35
  560.5 32.9 %collective-permute-start.4 = (bf16[128,1024]{0,1:T(8,128)(2,1)S(1)}, bf16[128,1024]{0,1:T(8,128)(2,1)S(1)}, u32[]{:S(2)}, u32[]{:S(2)}) collective-permute-start(bf16[128,1024]{0,1:T(8,128)(2,1)S(1)} %bitcast.269), channel_id=1, source_target_pairs={{0,16},{4,20},{8,24},{12,28},{16,32},{20,36},{24,40},{28,44},{32,4... | collective-permute-start | bytes 786440 | tf_op jit(solution)/shard_map/ppermute | solution.py:35
  570.0 24.9 %collective-permute-start.5 = (bf16[128,1024]{0,1:T(8,128)(2,1)S(1)}, bf16[128,1024]{0,1:T(8,128)(2,1)S(1)}, u32[]{:S(2)}, u32[]{:S(2)}) collective-permute-start(bf16[128,1024]{0,1:T(8,128)(2,1)S(1)} %bitcast.270), channel_id=1, source_target_pairs={{0,12},{4,16},{8,20},{12,24},{16,28},{20,32},{24,36},{28,40},{32,4... | collective-permute-start | bytes 786440 | tf_op jit(solution)/shard_map/ppermute | solution.py:35
  592.0 11.4 %collective-permute-start.6 = (bf16[128,1024]{0,1:T(8,128)(2,1)S(1)}, bf16[128,1024]{0,1:T(8,128)(2,1)S(1)}, u32[]{:S(2)}, u32[]{:S(2)}) collective-permute-start(bf16[128,1024]{0,1:T(8,128)(2,1)S(1)} %bitcast.271), channel_id=1, source_target_pairs={{0,8},{4,12},{8,16},{12,20},{16,24},{20,28},{24,32},{28,36},{32,40... | collective-permute-start | bytes 786440 | tf_op jit(solution)/shard_map/ppermute | solution.py:35
  593.4 21.8 %collective-permute-start.7 = (bf16[128,1024]{0,1:T(8,128)(2,1)S(1)}, bf16[128,1024]{0,1:T(8,128)(2,1)S(1)}, u32[]{:S(2)}, u32[]{:S(2)}) collective-permute-start(bf16[128,1024]{0,1:T(8,128)(2,1)S(1)} %bitcast.272), channel_id=1, source_target_pairs={{0,4},{4,8},{8,12},{12,16},{16,20},{20,24},{24,28},{28,32},{32,36}... | collective-permute-start | bytes 786440 | tf_op jit(solution)/shard_map/ppermute | solution.py:35
  594.8 44.4 %collective-permute-start.11 = (bf16[128,1024]{0,1:T(8,128)(2,1)S(1)}, bf16[128,1024]{0,1:T(8,128)(2,1)S(1)}, u32[]{:S(2)}, u32[]{:S(2)}) collective-permute-start(bf16[128,1024]{0,1:T(8,128)(2,1)S(1)} %bitcast.259), channel_id=1, source_target_pairs={{0,20},{4,24},{8,28},{12,32},{16,36},{20,40},{24,44},{28,48},{32,5... | collective-permute-start | bytes 786440 | tf_op jit(solution)/shard_map/ppermute | solution.py:35
  603.4 21.3 %collective-permute-start.9 = (bf16[128,1024]{0,1:T(8,128)(2,1)S(1)}, bf16[128,1024]{0,1:T(8,128)(2,1)S(1)}, u32[]{:S(2)}, u32[]{:S(2)}) collective-permute-start(bf16[128,1024]{0,1:T(8,128)(2,1)S(1)} %bitcast.260), channel_id=1, source_target_pairs={{0,28},{4,32},{8,36},{12,40},{16,44},{20,48},{24,52},{28,56},{32,6... | collective-permute-start | bytes 786440 | tf_op jit(solution)/shard_map/ppermute | solution.py:35
  615.2 22.4 %collective-permute-start.10 = (bf16[128,1024]{0,1:T(8,128)(2,1)S(1)}, bf16[128,1024]{0,1:T(8,128)(2,1)S(1)}, u32[]{:S(2)}, u32[]{:S(2)}) collective-permute-start(bf16[128,1024]{0,1:T(8,128)(2,1)S(1)} %bitcast.261), channel_id=1, source_target_pairs={{0,24},{4,28},{8,32},{12,36},{16,40},{20,44},{24,48},{28,52},{32,5... | collective-permute-start | bytes 786440 | tf_op jit(solution)/shard_map/ppermute | solution.py:35
  624.6 23.5 %copy-start.26 = (s32[128]{0:T(128)S(1)}, s32[128]{0:T(128)}, u32[]{:S(2)}) copy-start(s32[128]{0:T(128)} %compare_select_fusion) | copy-start | bytes 1540
  624.6 23.5 %copy-start.28 = (s32[128]{0:T(128)S(1)}, s32[128]{0:T(128)}, u32[]{:S(2)}) copy-start(s32[128]{0:T(128)} %get-tuple-element.461) | copy-start | bytes 1540
  624.7 22.0 %copy-start.5 = (bf16[1152,4,2,128]{0,3,2,1:T(8,128)(2,1)}, bf16[1152,4,2,128]{0,3,2,1:T(8,128)(2,1)S(1)}, u32[]{:S(2)}) copy-start(bf16[1152,4,2,128]{0,3,2,1:T(8,128)(2,1)S(1)} %constant_dynamic-update-slice_fusion) | copy-start | bytes 7077892
  624.7 17.3 %collective-permute-start.12 = (bf16[128,1024]{0,1:T(8,128)(2,1)S(1)}, bf16[128,1024]{0,1:T(8,128)(2,1)S(1)}, u32[]{:S(2)}, u32[]{:S(2)}) collective-permute-start(bf16[128,1024]{0,1:T(8,128)(2,1)S(1)} %bitcast.262), channel_id=1, source_target_pairs={{0,16},{4,20},{8,24},{12,28},{16,32},{20,36},{24,40},{28,44},{32,4... | collective-permute-start | bytes 786440 | tf_op jit(solution)/shard_map/ppermute | solution.py:35
  637.6 8.8 collective-permute-start.13
  718.0 3.5 copy-start.11
  727.4 31.2 %collective-permute-start.23 = (bf16[128,1024]{0,1:T(8,128)(2,1)}, bf16[128,1024]{0,1:T(8,128)(2,1)}, u32[]{:S(2)}, u32[]{:S(2)}) collective-permute-start(bf16[128,1024]{0,1:T(8,128)(2,1)} %bitcast.46), channel_id=1, source_target_pairs={{32,0},{36,4},{40,8},{44,12},{48,16},{52,20},{56,24},{60,28},{64,3... | collective-permute-start | bytes 786440 | tf_op jit(solution)/shard_map/ppermute | solution.py:35
  728.6 31.2 %collective-permute-start.16 = (bf16[128,1024]{0,1:T(8,128)(2,1)}, bf16[128,1024]{0,1:T(8,128)(2,1)}, u32[]{:S(2)}, u32[]{:S(2)}) collective-permute-start(bf16[128,1024]{0,1:T(8,128)(2,1)} %bitcast.39), channel_id=1, source_target_pairs={{4,0},{8,4},{12,8},{16,12},{20,16},{24,20},{28,24},{32,28},{36,32}... | collective-permute-start | bytes 786440 | tf_op jit(solution)/shard_map/ppermute | solution.py:35
  729.9 69.9 %collective-permute-start.22 = (bf16[128,1024]{0,1:T(8,128)(2,1)}, bf16[128,1024]{0,1:T(8,128)(2,1)}, u32[]{:S(2)}, u32[]{:S(2)}) collective-permute-start(bf16[128,1024]{0,1:T(8,128)(2,1)} %bitcast.45), channel_id=1, source_target_pairs={{28,0},{32,4},{36,8},{40,12},{44,16},{48,20},{52,24},{56,28},{60,3... | collective-permute-start | bytes 786440 | tf_op jit(solution)/shard_map/ppermute | solution.py:35
  735.1 74.6 %collective-permute-start.21 = (bf16[128,1024]{0,1:T(8,128)(2,1)}, bf16[128,1024]{0,1:T(8,128)(2,1)S(1)}, u32[]{:S(2)}, u32[]{:S(2)}) collective-permute-start(bf16[128,1024]{0,1:T(8,128)(2,1)} %bitcast.278), channel_id=1, source_target_pairs={{24,0},{28,4},{32,8},{36,12},{40,16},{44,20},{48,24},{52,28},{56,3... | collective-permute-start | bytes 786440 | tf_op jit(solution)/shard_map/ppermute | solution.py:35
  736.4 74.6 %collective-permute-start.20 = (bf16[128,1024]{0,1:T(8,128)(2,1)}, bf16[128,1024]{0,1:T(8,128)(2,1)S(1)}, u32[]{:S(2)}, u32[]{:S(2)}) collective-permute-start(bf16[128,1024]{0,1:T(8,128)(2,1)} %bitcast.277), channel_id=1, source_target_pairs={{20,0},{24,4},{28,8},{32,12},{36,16},{40,20},{44,24},{48,28},{52,3... | collective-permute-start | bytes 786440 | tf_op jit(solution)/shard_map/ppermute | solution.py:35
  758.5 53.7 %collective-permute-start.19 = (bf16[128,1024]{0,1:T(8,128)(2,1)}, bf16[128,1024]{0,1:T(8,128)(2,1)S(1)}, u32[]{:S(2)}, u32[]{:S(2)}) collective-permute-start(bf16[128,1024]{0,1:T(8,128)(2,1)} %bitcast.276), channel_id=1, source_target_pairs={{16,0},{20,4},{24,8},{28,12},{32,16},{36,20},{40,24},{44,28},{48,3... | collective-permute-start | bytes 786440 | tf_op jit(solution)/shard_map/ppermute | solution.py:35
  759.8 53.7 %collective-permute-start.18 = (bf16[128,1024]{0,1:T(8,128)(2,1)}, bf16[128,1024]{0,1:T(8,128)(2,1)}, u32[]{:S(2)}, u32[]{:S(2)}) collective-permute-start(bf16[128,1024]{0,1:T(8,128)(2,1)} %bitcast.275), channel_id=1, source_target_pairs={{12,0},{16,4},{20,8},{24,12},{28,16},{32,20},{36,24},{40,28},{44,3... | collective-permute-start | bytes 786440 | tf_op jit(solution)/shard_map/ppermute | solution.py:35
  799.8 15.1 %collective-permute-start.17 = (bf16[128,1024]{0,1:T(8,128)(2,1)}, bf16[128,1024]{0,1:T(8,128)(2,1)}, u32[]{:S(2)}, u32[]{:S(2)}) collective-permute-start(bf16[128,1024]{0,1:T(8,128)(2,1)} %bitcast.274), channel_id=1, source_target_pairs={{8,0},{12,4},{16,8},{20,12},{24,16},{28,20},{32,24},{36,28},{40,32... | collective-permute-start | bytes 786440 | tf_op jit(solution)/shard_map/ppermute | solution.py:35
  802.8 13.4 %copy-start.7 = (f32[128,4,2,128]{0,3,2,1:T(8,128)S(1)}, f32[128,4,2,128]{0,3,2,1:T(8,128)}, u32[]{:S(2)}) copy-start(f32[128,4,2,128]{0,3,2,1:T(8,128)} %slice.144) | copy-start | bytes 1572868
  809.6 16.5 %collective-permute-start.25 = (bf16[128,1024]{1,0:T(8,128)(2,1)}, bf16[128,1024]{1,0:T(8,128)(2,1)}, u32[]{:S(2)}, u32[]{:S(2)}) collective-permute-start(bf16[128,1024]{1,0:T(8,128)(2,1)} %copy.218), channel_id=1, source_target_pairs={{8,0},{12,4},{16,8},{20,12},{24,16},{28,20},{32,24},{36,28},{40,32... | collective-permute-start | bytes 786440 | tf_op jit(solution)/shard_map/ppermute | solution.py:35
  810.9 21.1 %collective-permute-start.26 = (bf16[128,1024]{1,0:T(8,128)(2,1)}, bf16[128,1024]{1,0:T(8,128)(2,1)}, u32[]{:S(2)}, u32[]{:S(2)}) collective-permute-start(bf16[128,1024]{1,0:T(8,128)(2,1)} %copy.219), channel_id=1, source_target_pairs={{12,0},{16,4},{20,8},{24,12},{28,16},{32,20},{36,24},{40,28},{44,3... | collective-permute-start | bytes 786440 | tf_op jit(solution)/shard_map/ppermute | solution.py:35
  812.2 21.1 %collective-permute-start.27 = (bf16[128,1024]{1,0:T(8,128)(2,1)}, bf16[128,1024]{1,0:T(8,128)(2,1)}, u32[]{:S(2)}, u32[]{:S(2)}) collective-permute-start(bf16[128,1024]{1,0:T(8,128)(2,1)} %copy.220), channel_id=1, source_target_pairs={{16,0},{20,4},{24,8},{28,12},{32,16},{36,20},{40,24},{44,28},{48,3... | collective-permute-start | bytes 786440 | tf_op jit(solution)/shard_map/ppermute | solution.py:35
  813.6 247.2 %collective-permute-start.28 = (bf16[128,1024]{1,0:T(8,128)(2,1)}, bf16[128,1024]{1,0:T(8,128)(2,1)}, u32[]{:S(2)}, u32[]{:S(2)}) collective-permute-start(bf16[128,1024]{1,0:T(8,128)(2,1)} %copy.221), channel_id=1, source_target_pairs={{20,0},{24,4},{28,8},{32,12},{36,16},{40,20},{44,24},{48,28},{52,3... | collective-permute-start | bytes 786440 | tf_op jit(solution)/shard_map/ppermute | solution.py:35
  814.9 245.9 %collective-permute-start.29 = (bf16[128,1024]{1,0:T(8,128)(2,1)}, bf16[128,1024]{1,0:T(8,128)(2,1)}, u32[]{:S(2)}, u32[]{:S(2)}) collective-permute-start(bf16[128,1024]{1,0:T(8,128)(2,1)} %copy.222), channel_id=1, source_target_pairs={{24,0},{28,4},{32,8},{36,12},{40,16},{44,20},{48,24},{52,28},{56,3... | collective-permute-start | bytes 786440 | tf_op jit(solution)/shard_map/ppermute | solution.py:35
  818.3 13.7 %copy-start.21 = (bf16[128,1024]{1,0:T(8,128)(2,1)S(1)}, bf16[128,1024]{1,0:T(8,128)(2,1)}, u32[]{:S(2)}) copy-start(bf16[128,1024]{1,0:T(8,128)(2,1)} %copy.224) | copy-start | bytes 786436
  818.3 15.0 %copy-start.20 = (bf16[128,1024]{1,0:T(8,128)(2,1)S(1)}, bf16[128,1024]{1,0:T(8,128)(2,1)}, u32[]{:S(2)}) copy-start(bf16[128,1024]{1,0:T(8,128)(2,1)} %copy.217) | copy-start | bytes 786436
  818.3 16.3 %copy-start.25 = (f32[128,8]{0,1:T(8,128)S(1)}, f32[128,8]{0,1:T(8,128)}, u32[]{:S(2)}) copy-start(f32[128,8]{0,1:T(8,128)} %copy-done.24) | copy-start | bytes 12292
  818.8 242.0 %copy-start.6 = (f32[128,1024]{1,0:T(8,128)S(1)}, f32[128,1024]{1,0:T(8,128)}, u32[]{:S(2)}) copy-start(f32[128,1024]{1,0:T(8,128)} %copy.216) | copy-start | bytes 1572868
  826.2 234.6 %collective-permute-start.30 = (bf16[128,1024]{1,0:T(8,128)(2,1)}, bf16[128,1024]{1,0:T(8,128)(2,1)S(1)}, u32[]{:S(2)}, u32[]{:S(2)}) collective-permute-start(bf16[128,1024]{1,0:T(8,128)(2,1)} %copy.223), channel_id=1, source_target_pairs={{28,0},{32,4},{36,8},{40,12},{44,16},{48,20},{52,24},{56,28},{60,3... | collective-permute-start | bytes 786440 | tf_op jit(solution)/shard_map/ppermute | solution.py:35
  832.0 228.8 %collective-permute-start.31 = (bf16[128,1024]{1,0:T(8,128)(2,1)S(1)}, bf16[128,1024]{1,0:T(8,128)(2,1)}, u32[]{:S(2)}, u32[]{:S(2)}) collective-permute-start(bf16[128,1024]{1,0:T(8,128)(2,1)S(1)} %copy-done.21), channel_id=1, source_target_pairs={{32,0},{36,4},{40,8},{44,12},{48,16},{52,20},{56,24},{60,28},{64,3... | collective-permute-start | bytes 786440 | tf_op jit(solution)/shard_map/ppermute | solution.py:35
  833.3 227.5 %collective-permute-start.24 = (bf16[128,1024]{1,0:T(8,128)(2,1)S(1)}, bf16[128,1024]{1,0:T(8,128)(2,1)}, u32[]{:S(2)}, u32[]{:S(2)}) collective-permute-start(bf16[128,1024]{1,0:T(8,128)(2,1)S(1)} %copy-done.20), channel_id=1, source_target_pairs={{4,0},{8,4},{12,8},{16,12},{20,16},{24,20},{28,24},{32,28},{36,32}... | collective-permute-start | bytes 786440 | tf_op jit(solution)/shard_map/ppermute | solution.py:35
  (37 other events, 69.9 us)
where the time goes:
time: 1080 us; the launch traced here: 1060 us
  loops' own time  337 us (31%)
  blocking collectives  253 us (23%)
  local copies, waits for them, and re-layouts  192 us (18%)
  waiting for transfers between devices  107 us (10%)
  starting transfers between devices  99.1 us (9%)
  matrix products  48.5 us (4%)
  other arithmetic  24.7 us (2%)
    another operation x1, loops' own time, entering(): return lax.fori_loop(0, length, turn, start)  337 us
    psum x1, blocking collectives, shards(): lax.psum((query_gain_gradient, key_gain_gradient), ('seq', 'dp'))  225 us
    dynamic_slice x256, local copies, waits for them, and re-layouts, turn(): new = combine(before, jax.tree.map(lambda part: part[k], everything))  150 us
    ppermute x32, waiting for transfers between devices, from_behind(): lax.ppermute(value, axis, [(source, source + steps) for source in range(f...  107 us
    ppermute x32, starting transfers between devices, from_behind(): lax.ppermute(value, axis, [(source, source + steps) for source in range(f...  99.1 us
    all_gather x1, blocking collectives, entering(): everything = jax.tree.map(lambda part: lax.all_gather(part, axis), value)  28.4 us
  transfers between devices with their start and end apart: 32, of which 9 were waited for; matrix products, arithmetic and copies ran while one was open for 17% of the time, Pallas kernels for 0%

commit v1 on v0

--- a/solution.py
+++ b/solution.py
@@ -175,7 +175,7 @@
     key_raw_gradient, key_gain_gradient = key_backward(
         key_full_length.reshape(row_count, KEY_VALUE_HEADS, HEAD_SIZE)
     )
-    gain_query, gain_key = lax.psum((query_gain_gradient, key_gain_gradient), ("seq", "dp"))
+    gain_query, gain_key = lax.psum(lax.psum((query_gain_gradient, key_gain_gradient), "seq"), "dp")
     return (
         query_raw_gradient.astype(jnp.bfloat16).reshape(1, row_count, QUERY_HEADS * HEAD_SIZE),
         key_raw_gradient.astype(jnp.bfloat16).reshape(1, row_count, key_span_width),

time: 1080 us -> 1340 us (1.24)
  the two profiles are of different devices: /device:TPU:1 before, /device:TPU:264 now
where the time goes in v1:
time: 1340 us; the launch traced here: 1330 us
  blocking collectives  415 us (31%)
  loops' own time  337 us (25%)
  local copies, waits for them, and re-layouts  192 us (14%)
  starting transfers between devices  182 us (14%)
  waiting for transfers between devices  124 us (9%)
  matrix products  48.5 us (4%)
  other arithmetic  24.6 us (2%)
    psum x1, blocking collectives, shards(): lax.psum((query_gain_gradient, key_gain_gradient), 'seq')  381 us
    another operation x1, loops' own time, entering(): return lax.fori_loop(0, length, turn, start)  337 us
    ppermute x32, starting transfers between devices, from_behind(): lax.ppermute(value, axis, [(source, source + steps) for source in range(f...  182 us
    dynamic_slice x256, local copies, waits for them, and re-layouts, turn(): new = combine(before, jax.tree.map(lambda part: part[k], everything))  150 us
    ppermute x32, waiting for transfers between devices, from_behind(): lax.ppermute(value, axis, [(source, source + steps) for source in range(f...  124 us
    all_gather x1, blocking collectives, entering(): everything = jax.tree.map(lambda part: lax.all_gather(part, axis), value)  27.8 us
  transfers between devices with their start and end apart: 32, of which 12 were waited for; matrix products, arithmetic and copies ran while one was open for 14% of the time, Pallas kernels for 0%

profile of v1, /device:TPU:264, one launch (start us, length us, event | category | flops | bytes accessed | tf_op | source)
XLA Modules:
  0.0 1325.1 jit_solution(6588641132423515834)
XLA Ops:
  1.8 3.5 collective-permute-start.15
  5.3 5.7 collective-permute-start.14
  11.0 3.4 collective-permute-start.8
  17.7 2.1 collective-permute-start.1
  19.8 3.2 collective-permute-start
  27.2 27.8 %all-reduce.6 = (s32[128]{0:T(128)S(1)}, s32[128]{0:T(128)S(1)}) all-reduce(s32[128]{0:T(128)S(1)} %bitcast_dynamic-update-slice_fusion, s32[128]{0:T(128)S(1)} %slice_dynamic-update-slice_fusion), channel_id=2, replica_groups=mesh['seq'=128,'dp'=4] {'seq'}, use_global_device_ids=true, to_apply=%add.4 | all-reduce | flops 256 | bytes 2048 | tf_op jit(solution)/shard_map/all_gather | solution.py:17
  55.0 487.3 %while.30 = (s32[]{:T(128)}, s32[]{:T(128)}, s32[]{:T(128)}, s32[]{:T(128)}, s32[128]{0:T(128)S(1)}, /*index=5*/s32[128]{0:T(128)S(1)}, s32[]{:T(128)}, s32[]{:T(128)}) while((s32[]{:T(128)}, s32[]{:T(128)}, s32[]{:T(128)}, s32[]{:T(128)}, s32[128]{0:T(128)S(1)}, /*index=5*/s32[128]{0:T(128)S(1)}, s32[]{:T(128)}, s32[]{:T(128)}) %tuple.77), condition=%wide.region_4.5_spmd, body=%wide.region_3.4_spmd.sunk | while | flops 10 | bytes 199 | solution.py:29
  546.2 3.9 collective-permute-start.2
  551.2 11.3 collective-permute-start.3
  565.5 4.9 collective-permute-done.2
  570.4 13.5 %collective-permute-start.5 = (bf16[128,1024]{0,1:T(8,128)(2,1)S(1)}, bf16[128,1024]{0,1:T(8,128)(2,1)S(1)}, u32[]{:S(2)}, u32[]{:S(2)}) collective-permute-start(bf16[128,1024]{0,1:T(8,128)(2,1)S(1)} %bitcast.270), channel_id=1, source_target_pairs={{0,12},{4,16},{8,20},{12,24},{16,28},{20,32},{24,36},{28,40},{32,4... | collective-permute-start | bytes 786440 | tf_op jit(solution)/shard_map/ppermute | solution.py:35
  584.9 8.5 collective-permute-start.6
  593.4 9.8 collective-permute-done.4
  603.2 3.1 collective-permute-start.7
  606.3 6.2 collective-permute-done.5
  614.6 8.2 collective-permute-done.6
  626.8 34.6 %collective-permute-done.9 = bf16[128,1024]{0,1:T(8,128)(2,1)S(1)} collective-permute-done((bf16[128,1024]{0,1:T(8,128)(2,1)S(1)}, bf16[128,1024]{0,1:T(8,128)(2,1)S(1)}, u32[]{:S(2)}, u32[]{:S(2)}) %collective-permute-start.9) | collective-permute-done | bytes 262176 | tf_op jit(solution)/shard_map/ppermute | solution.py:35
  663.4 2.1 collective-permute-start.13
  665.7 19.1 %collective-permute-done.12 = bf16[128,1024]{0,1:T(8,128)(2,1)S(1)} collective-permute-done((bf16[128,1024]{0,1:T(8,128)(2,1)S(1)}, bf16[128,1024]{0,1:T(8,128)(2,1)S(1)}, u32[]{:S(2)}, u32[]{:S(2)}) %collective-permute-start.12) | collective-permute-done | bytes 262176 | tf_op jit(solution)/shard_map/ppermute | solution.py:35
  684.9 6.3 collective-permute-done.13
  692.9 57.1 %while.31 = (s32[]{:T(128)}, f32[4,128,2,2,128]{1,4,3,2,0:T(8,128)}, f32[4,1152,2,128]{1,3,2,0:T(8,128)}, f32[4,1152,2,128]{1,3,2,0:T(8,128)}, bf16[4,1152,2,128...) while((s32[]{:T(128)}, ...), condition=%wide.region_7.8_spmd.clone, body=%wide.region_5.7_spmd.clone.sunk | while | flops 912131200 | bytes 24730428 | solution.py:158
  700.1 2.2 fusion.99
  702.3 2.4 fusion.101
  704.7 2.5 fusion.100
  714.4 2.2 fusion.99
  716.5 2.4 fusion.101
  718.9 2.5 fusion.100
  728.6 2.1 fusion.99
  730.8 2.5 fusion.101
  733.3 2.5 fusion.100
  743.0 2.1 fusion.99
  745.1 2.4 fusion.101
  747.6 2.5 fusion.100
  752.8 4.1 bitcast_convert_fusion.2
  758.7 4.1 bitcast_convert_fusion.1
  769.3 2.9 fusion.55
  774.1 9.7 collective-permute-start.16
  793.4 44.9 %collective-permute-start.19 = (bf16[128,1024]{0,1:T(8,128)(2,1)}, bf16[128,1024]{0,1:T(8,128)(2,1)S(1)}, u32[]{:S(2)}, u32[]{:S(2)}) collective-permute-start(bf16[128,1024]{0,1:T(8,128)(2,1)} %bitcast.276), channel_id=1, source_target_pairs={{16,0},{20,4},{24,8},{28,12},{32,16},{36,20},{40,24},{44,28},{48,3... | collective-permute-start | bytes 786440 | tf_op jit(solution)/shard_map/ppermute | solution.py:35
  840.3 15.0 %collective-permute-start.17 = (bf16[128,1024]{0,1:T(8,128)(2,1)}, bf16[128,1024]{0,1:T(8,128)(2,1)}, u32[]{:S(2)}, u32[]{:S(2)}) collective-permute-start(bf16[128,1024]{0,1:T(8,128)(2,1)} %bitcast.274), channel_id=1, source_target_pairs={{8,0},{12,4},{16,8},{20,12},{24,16},{28,20},{32,24},{36,28},{40,32... | collective-permute-start | bytes 786440 | tf_op jit(solution)/shard_map/ppermute | solution.py:35
  869.7 10.8 collective-permute-start.28
  880.5 10.8 collective-permute-done.17
  896.4 18.3 %collective-permute-done.25 = bf16[128,1024]{1,0:T(8,128)(2,1)} collective-permute-done((bf16[128,1024]{1,0:T(8,128)(2,1)}, bf16[128,1024]{1,0:T(8,128)(2,1)}, u32[]{:S(2)}, u32[]{:S(2)}) %collective-permute-start.25) | collective-permute-done | bytes 262176 | tf_op jit(solution)/shard_map/ppermute | solution.py:35
  916.5 2.6 collective-permute-done.26
  921.1 2.5 collective-permute-done.27
  923.6 10.4 collective-permute-start.24
  935.5 380.9 %all-reduce.7 = (f32[128]{0:T(128)S(1)}, f32[128]{0:T(128)S(1)}) all-reduce(f32[128]{0:T(128)S(1)} %get-tuple-element.251, f32[128]{0:T(128)S(1)} %get-tuple-element.253), channel_id=1, replica_groups=mesh['seq'=128,'dp'=4] {'seq'}, use_global_device_ids=true, to_apply=%region_11.12 | all-reduce | flops 256 | bytes 2048 | tf_op jit(solution)/shard_map/psum | solution.py:178
  1316.3 6.2 all-reduce.8
  1322.6 2.5 fusion.50
  (521 shorter events, 255.1 us)
Async XLA Ops:
  0.6 16.1 %copy-start.32 = (f32[128]{0:T(128)S(1)}, f32[128]{0:T(128)}, u32[]{:S(2)}) copy-start(f32[128]{0:T(128)} %param.17) | copy-start | bytes 1540
  1.8 689.6 %collective-permute-start.15 = (bf16[128,1024]{0,1:T(8,128)(2,1)S(1)}, bf16[128,1024]{0,1:T(8,128)(2,1)S(1)}, u32[]{:S(2)}, u32[]{:S(2)}) collective-permute-start(bf16[128,1024]{0,1:T(8,128)(2,1)S(1)} %bitcast.256), channel_id=1, source_target_pairs={{0,4},{4,8},{8,12},{12,16},{16,20},{20,24},{24,28},{28,32},{32,36}... | collective-permute-start | bytes 786440 | tf_op jit(solution)/shard_map/ppermute | solution.py:35
  5.3 686.0 %collective-permute-start.14 = (bf16[128,1024]{0,1:T(8,128)(2,1)S(1)}, bf16[128,1024]{0,1:T(8,128)(2,1)S(1)}, u32[]{:S(2)}, u32[]{:S(2)}) collective-permute-start(bf16[128,1024]{0,1:T(8,128)(2,1)S(1)} %bitcast.257), channel_id=1, source_target_pairs={{0,8},{4,12},{8,16},{12,20},{16,24},{20,28},{24,32},{28,36},{32,40... | collective-permute-start | bytes 786440 | tf_op jit(solution)/shard_map/ppermute | solution.py:35
  11.0 540.2 %collective-permute-start.8 = (bf16[128,1024]{0,1:T(8,128)(2,1)S(1)}, bf16[128,1024]{0,1:T(8,128)(2,1)S(1)}, u32[]{:S(2)}, u32[]{:S(2)}) collective-permute-start(bf16[128,1024]{0,1:T(8,128)(2,1)S(1)} %bitcast.258), channel_id=1, source_target_pairs={{0,32},{4,36},{8,40},{12,44},{16,48},{20,52},{24,56},{28,60},{32,6... | collective-permute-start | bytes 786440 | tf_op jit(solution)/shard_map/ppermute | solution.py:35
  16.2 6.8 copy-start.34
  16.3 526.0 %copy-start.16 = (bf16[1,128,2048]{2,1,0:T(8,128)(2,1)S(1)}, bf16[1,128,2048]{2,1,0:T(8,128)(2,1)}, u32[]{:S(2)}) copy-start(bf16[1,128,2048]{2,1,0:T(8,128)(2,1)} %param.11) | copy-start | bytes 1572868
  16.3 526.0 %copy-start.24 = (f32[128,8]{0,1:T(8,128)}, f32[128,8]{0,1:T(8,128)S(1)}, u32[]{:S(2)}) copy-start(f32[128,8]{0,1:T(8,128)S(1)} %copy.167) | copy-start | bytes 12292
  16.4 525.8 %copy-start.14 = (f32[128,8]{1,0:T(8,128)}, f32[128,8]{1,0:T(8,128)S(1)}, u32[]{:S(2)}) copy-start(f32[128,8]{1,0:T(8,128)S(1)} %copy.168) | copy-start | bytes 12292
  16.8 526.7 %copy-start.8 = (f32[128,64]{1,0:T(8,128)}, f32[128,64]{1,0:T(8,128)S(1)}, u32[]{:S(2)}) copy-start(f32[128,64]{1,0:T(8,128)S(1)} %get-tuple-element.323) | copy-start | bytes 98308
  16.8 526.7 %copy-start.10 = (f32[128,64]{1,0:T(8,128)}, f32[128,64]{1,0:T(8,128)S(1)}, u32[]{:S(2)}) copy-start(f32[128,64]{1,0:T(8,128)S(1)} %get-tuple-element.324) | copy-start | bytes 98308
  17.7 544.9 %collective-permute-start.1 = (bf16[128,1024]{0,1:T(8,128)(2,1)S(1)}, bf16[128,1024]{0,1:T(8,128)(2,1)}, u32[]{:S(2)}, u32[]{:S(2)}) collective-permute-start(bf16[128,1024]{0,1:T(8,128)(2,1)S(1)} %bitcast.265), channel_id=1, source_target_pairs={{0,28},{4,32},{8,36},{12,40},{16,44},{20,48},{24,52},{28,56},{32,6... | collective-permute-start | bytes 786440 | tf_op jit(solution)/shard_map/ppermute | solution.py:35
  19.8 526.5 %collective-permute-start = (bf16[128,1024]{0,1:T(8,128)(2,1)S(1)}, bf16[128,1024]{0,1:T(8,128)(2,1)}, u32[]{:S(2)}, u32[]{:S(2)}) collective-permute-start(bf16[128,1024]{0,1:T(8,128)(2,1)S(1)} %bitcast.266), channel_id=1, source_target_pairs={{0,32},{4,36},{8,40},{12,44},{16,48},{20,52},{24,56},{28,60},{32,6... | collective-permute-start | bytes 786440 | tf_op jit(solution)/shard_map/ppermute | solution.py:35
  546.2 24.2 %collective-permute-start.2 = (bf16[128,1024]{0,1:T(8,128)(2,1)S(1)}, bf16[128,1024]{0,1:T(8,128)(2,1)S(1)}, u32[]{:S(2)}, u32[]{:S(2)}) collective-permute-start(bf16[128,1024]{0,1:T(8,128)(2,1)S(1)} %bitcast.267), channel_id=1, source_target_pairs={{0,24},{4,28},{8,32},{12,36},{16,40},{20,44},{24,48},{28,52},{32,5... | collective-permute-start | bytes 786440 | tf_op jit(solution)/shard_map/ppermute | solution.py:35
  551.2 33.7 %collective-permute-start.3 = (bf16[128,1024]{0,1:T(8,128)(2,1)S(1)}, bf16[128,1024]{0,1:T(8,128)(2,1)S(1)}, u32[]{:S(2)}, u32[]{:S(2)}) collective-permute-start(bf16[128,1024]{0,1:T(8,128)(2,1)S(1)} %bitcast.268), channel_id=1, source_target_pairs={{0,20},{4,24},{8,28},{12,32},{16,36},{20,40},{24,44},{28,48},{32,5... | collective-permute-start | bytes 786440 | tf_op jit(solution)/shard_map/ppermute | solution.py:35
  562.6 40.6 %collective-permute-start.4 = (bf16[128,1024]{0,1:T(8,128)(2,1)S(1)}, bf16[128,1024]{0,1:T(8,128)(2,1)S(1)}, u32[]{:S(2)}, u32[]{:S(2)}) collective-permute-start(bf16[128,1024]{0,1:T(8,128)(2,1)S(1)} %bitcast.269), channel_id=1, source_target_pairs={{0,16},{4,20},{8,24},{12,28},{16,32},{20,36},{24,40},{28,44},{32,4... | collective-permute-start | bytes 786440 | tf_op jit(solution)/shard_map/ppermute | solution.py:35
  570.4 42.2 %collective-permute-start.5 = (bf16[128,1024]{0,1:T(8,128)(2,1)S(1)}, bf16[128,1024]{0,1:T(8,128)(2,1)S(1)}, u32[]{:S(2)}, u32[]{:S(2)}) collective-permute-start(bf16[128,1024]{0,1:T(8,128)(2,1)S(1)} %bitcast.270), channel_id=1, source_target_pairs={{0,12},{4,16},{8,20},{12,24},{16,28},{20,32},{24,36},{28,40},{32,4... | collective-permute-start | bytes 786440 | tf_op jit(solution)/shard_map/ppermute | solution.py:35
  584.9 37.9 %collective-permute-start.6 = (bf16[128,1024]{0,1:T(8,128)(2,1)S(1)}, bf16[128,1024]{0,1:T(8,128)(2,1)S(1)}, u32[]{:S(2)}, u32[]{:S(2)}) collective-permute-start(bf16[128,1024]{0,1:T(8,128)(2,1)S(1)} %bitcast.271), channel_id=1, source_target_pairs={{0,8},{4,12},{8,16},{12,20},{16,24},{20,28},{24,32},{28,36},{32,40... | collective-permute-start | bytes 786440 | tf_op jit(solution)/shard_map/ppermute | solution.py:35
  603.2 21.5 %collective-permute-start.7 = (bf16[128,1024]{0,1:T(8,128)(2,1)S(1)}, bf16[128,1024]{0,1:T(8,128)(2,1)S(1)}, u32[]{:S(2)}, u32[]{:S(2)}) collective-permute-start(bf16[128,1024]{0,1:T(8,128)(2,1)S(1)} %bitcast.272), channel_id=1, source_target_pairs={{0,4},{4,8},{8,12},{12,16},{16,20},{20,24},{24,28},{28,32},{32,36}... | collective-permute-start | bytes 786440 | tf_op jit(solution)/shard_map/ppermute | solution.py:35
  612.6 53.0 %collective-permute-start.11 = (bf16[128,1024]{0,1:T(8,128)(2,1)S(1)}, bf16[128,1024]{0,1:T(8,128)(2,1)S(1)}, u32[]{:S(2)}, u32[]{:S(2)}) collective-permute-start(bf16[128,1024]{0,1:T(8,128)(2,1)S(1)} %bitcast.259), channel_id=1, source_target_pairs={{0,20},{4,24},{8,28},{12,32},{16,36},{20,40},{24,44},{28,48},{32,5... | collective-permute-start | bytes 786440 | tf_op jit(solution)/shard_map/ppermute | solution.py:35
  622.7 38.7 %collective-permute-start.9 = (bf16[128,1024]{0,1:T(8,128)(2,1)S(1)}, bf16[128,1024]{0,1:T(8,128)(2,1)S(1)}, u32[]{:S(2)}, u32[]{:S(2)}) collective-permute-start(bf16[128,1024]{0,1:T(8,128)(2,1)S(1)} %bitcast.260), channel_id=1, source_target_pairs={{0,28},{4,32},{8,36},{12,40},{16,44},{20,48},{24,52},{28,56},{32,6... | collective-permute-start | bytes 786440 | tf_op jit(solution)/shard_map/ppermute | solution.py:35
  624.7 38.7 %collective-permute-start.10 = (bf16[128,1024]{0,1:T(8,128)(2,1)S(1)}, bf16[128,1024]{0,1:T(8,128)(2,1)S(1)}, u32[]{:S(2)}, u32[]{:S(2)}) collective-permute-start(bf16[128,1024]{0,1:T(8,128)(2,1)S(1)} %bitcast.261), channel_id=1, source_target_pairs={{0,24},{4,28},{8,32},{12,36},{16,40},{20,44},{24,48},{28,52},{32,5... | collective-permute-start | bytes 786440 | tf_op jit(solution)/shard_map/ppermute | solution.py:35
  626.7 66.2 %copy-start.26 = (s32[128]{0:T(128)S(1)}, s32[128]{0:T(128)}, u32[]{:S(2)}) copy-start(s32[128]{0:T(128)} %compare_select_fusion) | copy-start | bytes 1540
  626.7 66.2 %copy-start.28 = (s32[128]{0:T(128)S(1)}, s32[128]{0:T(128)}, u32[]{:S(2)}) copy-start(s32[128]{0:T(128)} %get-tuple-element.463) | copy-start | bytes 1540
  626.8 64.7 %copy-start.5 = (bf16[1152,4,2,128]{0,3,2,1:T(8,128)(2,1)}, bf16[1152,4,2,128]{0,3,2,1:T(8,128)(2,1)S(1)}, u32[]{:S(2)}) copy-start(bf16[1152,4,2,128]{0,3,2,1:T(8,128)(2,1)S(1)} %constant_dynamic-update-slice_fusion) | copy-start | bytes 7077892
  661.4 23.3 %collective-permute-start.12 = (bf16[128,1024]{0,1:T(8,128)(2,1)S(1)}, bf16[128,1024]{0,1:T(8,128)(2,1)S(1)}, u32[]{:S(2)}, u32[]{:S(2)}) collective-permute-start(bf16[128,1024]{0,1:T(8,128)(2,1)S(1)} %bitcast.262), channel_id=1, source_target_pairs={{0,16},{4,20},{8,24},{12,28},{16,32},{20,36},{24,40},{28,44},{32,4... | collective-permute-start | bytes 786440 | tf_op jit(solution)/shard_map/ppermute | solution.py:35
  663.4 27.7 %collective-permute-start.13 = (bf16[128,1024]{0,1:T(8,128)(2,1)S(1)}, bf16[128,1024]{0,1:T(8,128)(2,1)S(1)}, u32[]{:S(2)}, u32[]{:S(2)}) collective-permute-start(bf16[128,1024]{0,1:T(8,128)(2,1)S(1)} %bitcast.263), channel_id=1, source_target_pairs={{0,12},{4,16},{8,20},{12,24},{16,28},{20,32},{24,36},{28,40},{32,4... | collective-permute-start | bytes 786440 | tf_op jit(solution)/shard_map/ppermute | solution.py:35
  762.8 3.5 copy-start.11
  772.2 21.3 %collective-permute-start.23 = (bf16[128,1024]{0,1:T(8,128)(2,1)}, bf16[128,1024]{0,1:T(8,128)(2,1)}, u32[]{:S(2)}, u32[]{:S(2)}) collective-permute-start(bf16[128,1024]{0,1:T(8,128)(2,1)} %bitcast.46), channel_id=1, source_target_pairs={{32,0},{36,4},{40,8},{44,12},{48,16},{52,20},{56,24},{60,28},{64,3... | collective-permute-start | bytes 786440 | tf_op jit(solution)/shard_map/ppermute | solution.py:35
  774.1 64.3 %collective-permute-start.16 = (bf16[128,1024]{0,1:T(8,128)(2,1)}, bf16[128,1024]{0,1:T(8,128)(2,1)}, u32[]{:S(2)}, u32[]{:S(2)}) collective-permute-start(bf16[128,1024]{0,1:T(8,128)(2,1)} %bitcast.39), channel_id=1, source_target_pairs={{4,0},{8,4},{12,8},{16,12},{20,16},{24,20},{28,24},{32,28},{36,32}... | collective-permute-start | bytes 786440 | tf_op jit(solution)/shard_map/ppermute | solution.py:35
  783.8 56.5 %collective-permute-start.22 = (bf16[128,1024]{0,1:T(8,128)(2,1)}, bf16[128,1024]{0,1:T(8,128)(2,1)}, u32[]{:S(2)}, u32[]{:S(2)}) collective-permute-start(bf16[128,1024]{0,1:T(8,128)(2,1)} %bitcast.45), channel_id=1, source_target_pairs={{28,0},{32,4},{36,8},{40,12},{44,16},{48,20},{52,24},{56,28},{60,3... | collective-permute-start | bytes 786440 | tf_op jit(solution)/shard_map/ppermute | solution.py:35
  789.6 74.3 %collective-permute-start.21 = (bf16[128,1024]{0,1:T(8,128)(2,1)}, bf16[128,1024]{0,1:T(8,128)(2,1)S(1)}, u32[]{:S(2)}, u32[]{:S(2)}) collective-permute-start(bf16[128,1024]{0,1:T(8,128)(2,1)} %bitcast.278), channel_id=1, source_target_pairs={{24,0},{28,4},{32,8},{36,12},{40,16},{44,20},{48,24},{52,28},{56,3... | collective-permute-start | bytes 786440 | tf_op jit(solution)/shard_map/ppermute | solution.py:35
  791.5 74.3 %collective-permute-start.20 = (bf16[128,1024]{0,1:T(8,128)(2,1)}, bf16[128,1024]{0,1:T(8,128)(2,1)S(1)}, u32[]{:S(2)}, u32[]{:S(2)}) collective-permute-start(bf16[128,1024]{0,1:T(8,128)(2,1)} %bitcast.277), channel_id=1, source_target_pairs={{20,0},{24,4},{28,8},{32,12},{36,16},{40,20},{44,24},{48,28},{52,3... | collective-permute-start | bytes 786440 | tf_op jit(solution)/shard_map/ppermute | solution.py:35
  793.4 74.3 %collective-permute-start.19 = (bf16[128,1024]{0,1:T(8,128)(2,1)}, bf16[128,1024]{0,1:T(8,128)(2,1)S(1)}, u32[]{:S(2)}, u32[]{:S(2)}) collective-permute-start(bf16[128,1024]{0,1:T(8,128)(2,1)} %bitcast.276), channel_id=1, source_target_pairs={{16,0},{20,4},{24,8},{28,12},{32,16},{36,20},{40,24},{44,28},{48,3... | collective-permute-start | bytes 786440 | tf_op jit(solution)/shard_map/ppermute | solution.py:35
  838.4 31.3 %collective-permute-start.18 = (bf16[128,1024]{0,1:T(8,128)(2,1)}, bf16[128,1024]{0,1:T(8,128)(2,1)}, u32[]{:S(2)}, u32[]{:S(2)}) collective-permute-start(bf16[128,1024]{0,1:T(8,128)(2,1)} %bitcast.275), channel_id=1, source_target_pairs={{12,0},{16,4},{20,8},{24,12},{28,16},{32,20},{36,24},{40,28},{44,3... | collective-permute-start | bytes 786440 | tf_op jit(solution)/shard_map/ppermute | solution.py:35
  840.3 51.0 %collective-permute-start.17 = (bf16[128,1024]{0,1:T(8,128)(2,1)}, bf16[128,1024]{0,1:T(8,128)(2,1)}, u32[]{:S(2)}, u32[]{:S(2)}) collective-permute-start(bf16[128,1024]{0,1:T(8,128)(2,1)} %bitcast.274), channel_id=1, source_target_pairs={{8,0},{12,4},{16,8},{20,12},{24,16},{28,20},{32,24},{36,28},{40,32... | collective-permute-start | bytes 786440 | tf_op jit(solution)/shard_map/ppermute | solution.py:35
  857.0 36.2 %copy-start.7 = (f32[128,4,2,128]{0,3,2,1:T(8,128)S(1)}, f32[128,4,2,128]{0,3,2,1:T(8,128)}, u32[]{:S(2)}) copy-start(f32[128,4,2,128]{0,3,2,1:T(8,128)} %slice.144) | copy-start | bytes 1572868
  863.9 50.8 %collective-permute-start.25 = (bf16[128,1024]{1,0:T(8,128)(2,1)}, bf16[128,1024]{1,0:T(8,128)(2,1)}, u32[]{:S(2)}, u32[]{:S(2)}) collective-permute-start(bf16[128,1024]{1,0:T(8,128)(2,1)} %copy.218), channel_id=1, source_target_pairs={{8,0},{12,4},{16,8},{20,12},{24,16},{28,20},{32,24},{36,28},{40,32... | collective-permute-start | bytes 786440 | tf_op jit(solution)/shard_map/ppermute | solution.py:35
  865.8 53.4 %collective-permute-start.26 = (bf16[128,1024]{1,0:T(8,128)(2,1)}, bf16[128,1024]{1,0:T(8,128)(2,1)}, u32[]{:S(2)}, u32[]{:S(2)}) collective-permute-start(bf16[128,1024]{1,0:T(8,128)(2,1)} %copy.219), channel_id=1, source_target_pairs={{12,0},{16,4},{20,8},{24,12},{28,16},{32,20},{36,24},{40,28},{44,3... | collective-permute-start | bytes 786440 | tf_op jit(solution)/shard_map/ppermute | solution.py:35
  867.7 55.9 %collective-permute-start.27 = (bf16[128,1024]{1,0:T(8,128)(2,1)}, bf16[128,1024]{1,0:T(8,128)(2,1)}, u32[]{:S(2)}, u32[]{:S(2)}) collective-permute-start(bf16[128,1024]{1,0:T(8,128)(2,1)} %copy.220), channel_id=1, source_target_pairs={{16,0},{20,4},{24,8},{28,12},{32,16},{36,20},{40,24},{44,28},{48,3... | collective-permute-start | bytes 786440 | tf_op jit(solution)/shard_map/ppermute | solution.py:35
  869.7 452.9 %collective-permute-start.28 = (bf16[128,1024]{1,0:T(8,128)(2,1)}, bf16[128,1024]{1,0:T(8,128)(2,1)}, u32[]{:S(2)}, u32[]{:S(2)}) collective-permute-start(bf16[128,1024]{1,0:T(8,128)(2,1)} %copy.221), channel_id=1, source_target_pairs={{20,0},{24,4},{28,8},{32,12},{36,16},{40,20},{44,24},{48,28},{52,3... | collective-permute-start | bytes 786440 | tf_op jit(solution)/shard_map/ppermute | solution.py:35
  891.3 431.3 %collective-permute-start.29 = (bf16[128,1024]{1,0:T(8,128)(2,1)}, bf16[128,1024]{1,0:T(8,128)(2,1)}, u32[]{:S(2)}, u32[]{:S(2)}) collective-permute-start(bf16[128,1024]{1,0:T(8,128)(2,1)} %copy.222), channel_id=1, source_target_pairs={{24,0},{28,4},{32,8},{36,12},{40,16},{44,20},{48,24},{52,28},{56,3... | collective-permute-start | bytes 786440 | tf_op jit(solution)/shard_map/ppermute | solution.py:35
  895.3 23.8 %copy-start.21 = (bf16[128,1024]{1,0:T(8,128)(2,1)S(1)}, bf16[128,1024]{1,0:T(8,128)(2,1)}, u32[]{:S(2)}) copy-start(bf16[128,1024]{1,0:T(8,128)(2,1)} %copy.224) | copy-start | bytes 786436
  895.3 28.3 %copy-start.20 = (bf16[128,1024]{1,0:T(8,128)(2,1)S(1)}, bf16[128,1024]{1,0:T(8,128)(2,1)}, u32[]{:S(2)}) copy-start(bf16[128,1024]{1,0:T(8,128)(2,1)} %copy.217) | copy-start | bytes 786436
  895.3 38.7 %copy-start.25 = (f32[128,8]{0,1:T(8,128)S(1)}, f32[128,8]{0,1:T(8,128)}, u32[]{:S(2)}) copy-start(f32[128,8]{0,1:T(8,128)} %copy-done.24) | copy-start | bytes 12292
  895.8 426.8 %copy-start.6 = (f32[128,1024]{1,0:T(8,128)S(1)}, f32[128,1024]{1,0:T(8,128)}, u32[]{:S(2)}) copy-start(f32[128,1024]{1,0:T(8,128)} %copy.216) | copy-start | bytes 1572868
  914.6 408.0 %collective-permute-start.30 = (bf16[128,1024]{1,0:T(8,128)(2,1)}, bf16[128,1024]{1,0:T(8,128)(2,1)S(1)}, u32[]{:S(2)}, u32[]{:S(2)}) collective-permute-start(bf16[128,1024]{1,0:T(8,128)(2,1)} %copy.223), channel_id=1, source_target_pairs={{28,0},{32,4},{36,8},{40,12},{44,16},{48,20},{52,24},{56,28},{60,3... | collective-permute-start | bytes 786440 | tf_op jit(solution)/shard_map/ppermute | solution.py:35
  919.2 403.4 %collective-permute-start.31 = (bf16[128,1024]{1,0:T(8,128)(2,1)S(1)}, bf16[128,1024]{1,0:T(8,128)(2,1)}, u32[]{:S(2)}, u32[]{:S(2)}) collective-permute-start(bf16[128,1024]{1,0:T(8,128)(2,1)S(1)} %copy-done.21), channel_id=1, source_target_pairs={{32,0},{36,4},{40,8},{44,12},{48,16},{52,20},{56,24},{60,28},{64,3... | collective-permute-start | bytes 786440 | tf_op jit(solution)/shard_map/ppermute | solution.py:35
  923.6 399.0 %collective-permute-start.24 = (bf16[128,1024]{1,0:T(8,128)(2,1)S(1)}, bf16[128,1024]{1,0:T(8,128)(2,1)}, u32[]{:S(2)}, u32[]{:S(2)}) collective-permute-start(bf16[128,1024]{1,0:T(8,128)(2,1)S(1)} %copy-done.20), channel_id=1, source_target_pairs={{4,0},{8,4},{12,8},{16,12},{20,16},{24,20},{28,24},{32,28},{36,32}... | collective-permute-start | bytes 786440 | tf_op jit(solution)/shard_map/ppermute | solution.py:35
  (37 other events, 69.9 us)
